TPU v7x, 128 devices: a whole 4x4x4 slice. The times are simulated.
128 devices in a mesh: node: 8 (over x, core), dev: 16 (over z, y).
Axes of the slice: x: 4, y: 4, z: 4, core: 2. Of those that a mesh axis runs over, the one named last changes fastest.
Arguments:
- tokens: bfloat16 [32768, 7168], P(('node', 'dev')), may hold values from -6 to 6
- grad_out: bfloat16 [32768, 7168], P(('node', 'dev')), may hold values from -1.796875 to 1.796875
- router_gates: bfloat16 [32768, 8], P(('node', 'dev')), may hold values from 0.049804688 to 1
- expert_ids: int32 [32768, 8], P(('node', 'dev')), may hold values from 0 to 255, as said below
- slot_plan: int32 [256, 2], replicated, may hold values from 0 to 16, as said below
- w_gate: bfloat16 [8, 7168, 2048], P(None, 'dev', 'node'), may hold values from -0.0625 to 0.0625
- w_up: bfloat16 [8, 7168, 2048], P(None, 'dev', 'node'), may hold values from -0.0625 to 0.0625
- w_down: bfloat16 [8, 2048, 7168], P(None, 'node', 'dev'), may hold values from -0.125 to 0.125
Outputs:
- grad_tokens: bfloat16 [32768, 7168], P(('node', 'dev'))
- grad_gates: float32 [32768, 8], P(('node', 'dev'))
- grad_w_gate: bfloat16 [8, 7168, 2048], P(None, 'dev', 'node')
- grad_w_up: bfloat16 [8, 7168, 2048], P(None, 'dev', 'node')
- grad_w_down: bfloat16 [8, 2048, 7168], P(None, 'node', 'dev')
Inputs may be any that keep to these rules, and one draw needn't show every extreme that they name: `expert_ids`: each token names 8 different experts. Within one block of 256 tokens (the tokens of one device), at most 4 pairs name any one expert that has slots, and in every draw one expert that has slots is named exactly 2 * 2 times in every block. `slot_plan`: exactly 8 rows hold slots: each such row holds two different slots, and every slot 0 .. 15 stands in exactly one row. Every entry of the other rows equals 16.
All inputs are finite; a program needn't handle non-finite values.
Results may differ from a plain program's by a relative error of at most 0.0059.
Values may be sent and summed in bfloat16 or wider, within the bound.
No kernel may reach another device: no remote copies, remote signals or barrier semaphores. Data moves between devices by JAX's collectives and lax.ppermute only.
A program may use at most 128 MiB of HBM per device.

v0:
```python
import jax
import jax.numpy as jnp
from jax import lax
from jax.sharding import PartitionSpec as P

EXPERTS = 256
TOP = 8
CAP = 2


def expert_pass(pieces, slot_gate, slot_up, slot_down):
    x_piece, dy_piece, gate_piece = pieces
    lead_count = x_piece.shape[0]
    slot_count = slot_down.shape[0]
    model_width = x_piece.shape[-1]
    x_rows = x_piece.reshape(-1, model_width)
    dy_split = dy_piece.reshape(-1, slot_count, model_width // slot_count)
    gate_rows = gate_piece.reshape(-1, 1).astype(jnp.float32)
    gate_pre = jnp.dot(x_rows, slot_gate, preferred_element_type=jnp.float32)
    up_pre = jnp.dot(x_rows, slot_up, preferred_element_type=jnp.float32)
    back_proj = jnp.einsum("rsk,shk->rh", dy_split, slot_down, preferred_element_type=jnp.float32)
    sigmoid_gate = jax.nn.sigmoid(gate_pre)
    active = gate_pre * sigmoid_gate
    hidden = active * up_pre
    scaled_back = gate_rows * back_proj
    d_gate = (scaled_back * up_pre * sigmoid_gate * (1.0 + gate_pre * (1.0 - sigmoid_gate))).astype(
        jnp.bfloat16
    )
    d_up = (scaled_back * active).astype(jnp.bfloat16)
    scaled_hidden = (gate_rows * hidden).astype(jnp.bfloat16)
    gate_terms = jnp.sum(back_proj * hidden, axis=-1)
    row_terms = jnp.einsum("rh,dh->rd", d_gate, slot_gate, preferred_element_type=jnp.float32)
    row_terms = row_terms + jnp.einsum(
        "rh,dh->rd", d_up, slot_up, preferred_element_type=jnp.float32
    )
    acc_gate = jnp.einsum("rd,rh->dh", x_rows, d_gate, preferred_element_type=jnp.float32)
    acc_up = jnp.einsum("rd,rh->dh", x_rows, d_up, preferred_element_type=jnp.float32)
    acc_down = jnp.einsum(
        "rsk,rh->shk", dy_split, scaled_hidden, preferred_element_type=jnp.float32
    )
    row_acc = row_terms.reshape(lead_count, slot_count, -1, model_width)
    gate_acc = gate_terms.reshape(lead_count, slot_count, -1)
    return (acc_gate, acc_up, acc_down, row_acc, gate_acc)


def local(tokens, grad_out, router_gates, expert_ids, slot_plan, w_gate, w_up, w_down):
    slot_count = lax.axis_size("dev")
    tok_rows, model_width = tokens.shape
    hidden_width = w_gate.shape[2]
    round_total = w_gate.shape[0]
    pair_total = tok_rows * TOP
    expert_match = expert_ids[:, :, None] == jnp.arange(EXPERTS, dtype=jnp.int32)
    first_slot = jnp.sum(jnp.where(expert_match, slot_plan[:, 0], 0), axis=-1).reshape(pair_total)
    second_slot = jnp.sum(jnp.where(expert_match, slot_plan[:, 1], 0), axis=-1).reshape(pair_total)
    is_live = first_slot < slot_count
    first_hot = (first_slot[:, None] == jnp.arange(slot_count, dtype=jnp.int32)[None, :]).astype(
        jnp.int32
    )
    pair_order = jnp.sum(first_hot * (jnp.cumsum(first_hot, axis=0) - 1), axis=-1)
    pair_slot = jnp.where(pair_order % 2 == 0, first_slot, second_slot)
    target_row = pair_slot * CAP + pair_order // 2
    position_ids = jnp.arange(slot_count * CAP, dtype=jnp.int32)
    chooser = (is_live[None, :] & (target_row[None, :] == position_ids[:, None])).astype(
        jnp.float32
    )
    pick_rows = jnp.sum(chooser.reshape(slot_count * CAP, tok_rows, TOP), axis=-1)
    pick_half = pick_rows.astype(jnp.bfloat16)
    x_send = (
        jnp.dot(pick_half, tokens, preferred_element_type=jnp.float32)
        .astype(jnp.bfloat16)
        .reshape(slot_count, CAP, model_width)
    )
    dy_send = (
        jnp.dot(pick_half, grad_out, preferred_element_type=jnp.float32)
        .astype(jnp.bfloat16)
        .reshape(slot_count, CAP, model_width)
    )
    flat_gates = router_gates.reshape(pair_total).astype(jnp.float32)
    gate_send = (
        jnp.dot(chooser, flat_gates, precision=lax.Precision.HIGHEST)
        .astype(jnp.bfloat16)
        .reshape(slot_count, CAP)
    )
    in_round = (slot_plan[:, 0] < slot_count).astype(jnp.int32)
    expert_rank = jnp.cumsum(in_round) - 1
    holder = jnp.any(slot_plan[:, :, None] == jnp.arange(slot_count, dtype=jnp.int32), axis=1)
    slot_rank = jnp.sum(jnp.where(holder, expert_rank[:, None], 0), axis=0)
    grouping = (slot_rank[None, :] == jnp.arange(round_total, dtype=jnp.int32)[:, None]).astype(
        jnp.bfloat16
    )
    copy_gate = jnp.take(w_gate, slot_rank, axis=0)
    copy_up = jnp.take(w_up, slot_rank, axis=0)
    copy_down = jnp.take(w_down, slot_rank, axis=0)
    slot_gate, slot_up, slot_down = (
        lax.all_to_all(copy_gate, "dev", split_axis=0, concat_axis=0, tiled=True),
        lax.all_to_all(copy_up, "dev", split_axis=0, concat_axis=0, tiled=True),
        lax.all_to_all(copy_down, "dev", split_axis=0, concat_axis=0, tiled=True),
    )
    slot_gate = slot_gate.reshape(model_width, hidden_width)
    slot_up = slot_up.reshape(model_width, hidden_width)
    got_x, got_dy, got_gate = (
        lax.all_to_all(x_send, "dev", split_axis=0, concat_axis=0, tiled=True),
        lax.all_to_all(dy_send, "dev", split_axis=0, concat_axis=0, tiled=True),
        lax.all_to_all(gate_send, "dev", split_axis=0, concat_axis=0, tiled=True),
    )
    totals = expert_pass(
        (
            lax.all_gather(got_x[None], "node", axis=0, tiled=True),
            lax.all_gather(got_dy[None], "node", axis=0, tiled=True),
            lax.all_gather(got_gate[None], "node", axis=0, tiled=True),
        ),
        slot_gate,
        slot_up,
        slot_down,
    )
    acc_gate, acc_up, acc_down, row_acc, gate_acc = totals
    summed_rows, summed_gates = (
        lax.psum_scatter(row_acc, "node", scatter_dimension=0, tiled=True),
        lax.psum_scatter(gate_acc, "node", scatter_dimension=0, tiled=True),
    )
    back_rows, back_gates = (
        lax.all_to_all(summed_rows, "dev", split_axis=1, concat_axis=1, tiled=True),
        lax.all_to_all(summed_gates, "dev", split_axis=1, concat_axis=1, tiled=True),
    )
    grad_tokens = jnp.einsum(
        "qt,qd->td",
        pick_rows,
        back_rows.reshape(slot_count * CAP, model_width),
        precision=lax.Precision.HIGHEST,
    ).astype(jnp.bfloat16)
    grad_gates = jnp.dot(
        back_gates.reshape(slot_count * CAP), chooser, precision=lax.Precision.HIGHEST
    ).reshape(tok_rows, TOP)
    send_gate = acc_gate.astype(jnp.bfloat16).reshape(
        slot_count, model_width // slot_count, hidden_width
    )
    send_up = acc_up.astype(jnp.bfloat16).reshape(
        slot_count, model_width // slot_count, hidden_width
    )
    send_down = acc_down.astype(jnp.bfloat16)
    got_wgate, got_wup, got_wdown = (
        lax.all_to_all(send_gate, "dev", split_axis=0, concat_axis=0, tiled=True),
        lax.all_to_all(send_up, "dev", split_axis=0, concat_axis=0, tiled=True),
        lax.all_to_all(send_down, "dev", split_axis=0, concat_axis=0, tiled=True),
    )
    grad_w_gate = jnp.einsum(
        "js,sdh->jdh", grouping, got_wgate, preferred_element_type=jnp.float32
    ).astype(jnp.bfloat16)
    grad_w_up = jnp.einsum(
        "js,sdh->jdh", grouping, got_wup, preferred_element_type=jnp.float32
    ).astype(jnp.bfloat16)
    grad_w_down = jnp.einsum(
        "js,shk->jhk", grouping, got_wdown, preferred_element_type=jnp.float32
    ).astype(jnp.bfloat16)
    return (grad_tokens, grad_gates, grad_w_gate, grad_w_up, grad_w_down)


def solution(mesh):
    return jax.shard_map(
        local,
        mesh=mesh,
        in_specs=(
            P(("node", "dev"), None),
            P(("node", "dev"), None),
            P(("node", "dev"), None),
            P(("node", "dev"), None),
            P(),
            P(None, "dev", "node"),
            P(None, "dev", "node"),
            P(None, "node", "dev"),
        ),
        out_specs=(
            P(("node", "dev"), None),
            P(("node", "dev"), None),
            P(None, "dev", "node"),
            P(None, "dev", "node"),
            P(None, "node", "dev"),
        ),
        check_vma=False,
    )
```

profile of v0, /device:TPU:14, one launch (start us, length us, event | category | flops | bytes accessed | tf_op | source)
XLA Modules:
  0.0 506.6 jit_solution(3346200505427443808)
XLA Ops:
  8.9 9.2 %select_reduce_fusion = (s32[256,8]{1,0:T(8,128)S(1)}, s32[256,8]{1,0:T(8,128)S(1)}) fusion(s32[256]{0:T(256)S(1)} %bitcast.78, s32[256,8]{1,0:T(8,128)S(1)} %copy.90, s32[256]{0:T(256)S(1)} %bitcast.77), kind=kLoop, calls=%fused_computation.21 | loop fusion | flops 2617344 | bytes 26624 | tf_op jit(solution)/shard_map/reduce_sum | solution.py:54
  27.2 17.7 %all_to_all.60 = bf16[16,2,7168]{2,1,0:T(2,128)(2,1)} all-to-all(bf16[16,2,7168]{2,1,0:T(2,128)(2,1)S(1)} %reshape.235), channel_id=1, replica_groups=mesh['node'=8,'dev'=16] {'dev'}, dimensions={0} | all-to-all | bytes 917504 | tf_op jit(solution)/shard_map/all_to_all | solution.py:102
  46.2 4.7 all-to-all-start
  62.3 7.3 %all-to-all-start.1 = ((bf16[16,2,7168]{2,1,0:T(2,128)(2,1)}), bf16[16,2,7168]{2,1,0:T(2,128)(2,1)S(1)}, u32[]{:S(2)}, u32[]{:S(2)}) async-start(bf16[16,2,7168]{2,1,0:T(2,128)(2,1)} %reshape.232), calls=%async_computation.1 | async-start | bytes 917504 | tf_op jit(solution)/shard_map/all_to_all | solution.py:103
  69.6 7.0 %broadcast_select_fusion.1 = (bf16[16,448,256]{2,1,0:T(8,128)(2,1)}, bf16[16,448,256]{2,1,0:T(8,128)(2,1)}) fusion(bf16[16,448,256]{2,1,0:T(8,128)(2,1)} %gather_fusion.1, pred[16]{0:T(512)(128)(4,1)S(1)} %compare_and_fusion, bf16[16,448,256]{2,1,0:T(8,128)(2,1)} %gather_fusion.2), kind=kLoop, calls=%fused_computation.19 | loop fusion | flops 3670016 | bytes 14680080 | tf_op jit(solution)/shard_map/jit(_take)/select_n | solution.py:92
  78.8 5.9 %all-to-all-start.5 = ((bf16[16,448,256]{2,1,0:T(8,128)(2,1)}), bf16[16,448,256]{2,1,0:T(8,128)(2,1)}, u32[]{:S(2)}, u32[]{:S(2)}) async-start(bf16[16,448,256]{2,1,0:T(8,128)(2,1)} %get-tuple-element.44), calls=%async_computation.5 | async-start | bytes 7340032 | tf_op jit(solution)/shard_map/all_to_all | solution.py:95
  85.4 44.8 %all-to-all-done.5 = bf16[16,448,256]{2,1,0:T(8,128)(2,1)} async-done(((bf16[16,448,256]{2,1,0:T(8,128)(2,1)}), bf16[16,448,256]{2,1,0:T(8,128)(2,1)}, u32[]{:S(2)}, u32[]{:S(2)}) %all-to-all-start.5) | async-done | bytes 3670048 | tf_op jit(solution)/shard_map/all_to_all | solution.py:95
  130.2 9.0 %all-to-all-start.4 = ((bf16[16,448,256]{2,1,0:T(8,128)(2,1)}), bf16[16,448,256]{2,1,0:T(8,128)(2,1)}, u32[]{:S(2)}, u32[]{:S(2)}) async-start(bf16[16,448,256]{2,1,0:T(8,128)(2,1)} %get-tuple-element.43), calls=%async_computation.4 | async-start | bytes 7340032 | tf_op jit(solution)/shard_map/all_to_all | solution.py:96
  146.2 38.6 %all-to-all-done.4 = bf16[16,448,256]{2,1,0:T(8,128)(2,1)} async-done(((bf16[16,448,256]{2,1,0:T(8,128)(2,1)}), bf16[16,448,256]{2,1,0:T(8,128)(2,1)}, u32[]{:S(2)}, u32[]{:S(2)}) %all-to-all-start.4) | async-done | bytes 3670048 | tf_op jit(solution)/shard_map/all_to_all | solution.py:96
  184.7 8.8 %all-to-all-start.2 = ((bf16[16,256,448]{1,2,0:T(8,128)(2,1)}), bf16[16,256,448]{1,2,0:T(8,128)(2,1)}, u32[]{:S(2)}, u32[]{:S(2)}) async-start(bf16[16,256,448]{1,2,0:T(8,128)(2,1)} %broadcast_select_fusion.2), calls=%async_computation.2 | async-start | bytes 7340032 | tf_op jit(solution)/shard_map/all_to_all | solution.py:97
  193.6 13.0 %all-gather = bf16[128,1,2]{2,1,0:T(2,128)(2,1)S(1)} all-gather(bf16[16,1,2]{2,1,0:T(2,128)(2,1)S(1)} %all-to-all-done), channel_id=2, replica_groups=mesh['node'=8,'dev'=16] {'node'}, dimensions={0}, use_global_device_ids=true | all-gather | bytes 576 | tf_op jit(solution)/shard_map/all_gather | solution.py:110
  206.9 8.4 %reshape.236 = bf16[256,7168]{1,0:T(8,128)(2,1)} reshape(bf16[128,2,7168]{2,1,0:T(2,128)(2,1)} %all-gather.8.cloned.1.call-done) | data formatting | bytes 7340032 | tf_op jit(solution)/shard_map/reshape | solution.py:16
  215.3 9.6 %reshape.233 = bf16[256,16,448]{2,1,0:T(8,128)(2,1)} reshape(bf16[128,2,7168]{2,1,0:T(2,128)(2,1)} %all-gather.6.cloned.1.call-done) | data formatting | bytes 7340032 | tf_op jit(solution)/shard_map/reshape | solution.py:17
  224.9 4.8 fusion.62
  233.4 5.7 %all-to-all-done.2 = bf16[16,256,448]{1,2,0:T(8,128)(2,1)} async-done(((bf16[16,256,448]{1,2,0:T(8,128)(2,1)}), bf16[16,256,448]{1,2,0:T(8,128)(2,1)}, u32[]{:S(2)}, u32[]{:S(2)}) %all-to-all-start.2) | async-done | bytes 3670048 | tf_op jit(solution)/shard_map/all_to_all | solution.py:97
  239.1 8.3 %multiply_reduce_fusion = (f32[256]{0:T(256)S(1)}, bf16[256,256]{0,1:T(8,128)(2,1)S(1)}, bf16[256,256]{0,1:T(8,128)(2,1)S(1)}) fusion(f32[256,256]{0,1:T(8,128)S(1)} %fusion.61, f32[256,256]{0,1:T(8,128)S(1)} %fusion.62, f32[256]{0:T(256)S(1)} %reshape.245, bf16[16,256,448]{1,2,0:T(8,128)(2,1)} %all-to-all-done.2, bf16[256,16,448]{2,1,0:T(8,128)(2,1)} %reshape.233), kind=kOutput, calls=%fused_computation.32 | convolution fusion | flops 940637952 | bytes 8128512 | tf_op jit(solution)/shard_map/rsk,shk->rh/dot_general | solution.py:21
  247.5 6.2 %fusion.63 = f32[256,7168]{1,0:T(8,128)} fusion(bf16[256,256]{0,1:T(8,128)(2,1)S(1)} %get-tuple-element.39, bf16[7168,256]{1,0:T(8,128)(2,1)} %bitcast.10), kind=kOutput, calls=%fused_computation.105 | convolution fusion | flops 939524096 | bytes 11141120 | tf_op jit(solution)/shard_map/rh,dh->rd/dot_general | solution.py:32
  254.5 8.3 %convolution_add_fusion = f32[256,7168]{1,0:T(8,128)} fusion(f32[256,7168]{1,0:T(8,128)} %fusion.63, bf16[256,256]{0,1:T(8,128)(2,1)S(1)} %get-tuple-element.40, bf16[7168,256]{1,0:T(8,128)(2,1)} %bitcast.9), kind=kOutput, calls=%fused_computation.3 | convolution fusion | flops 941359104 | bytes 18481152 | tf_op jit(solution)/shard_map/rh,dh->rd/dot_general | solution.py:33
  262.8 9.7 %reshape.239 = f32[8,16,2,7168]{3,2,1,0:T(2,128)} reshape(f32[256,7168]{1,0:T(8,128)} %convolution_add_fusion) | data formatting | bytes 14680064 | tf_op jit(solution)/shard_map/reshape | solution.py:41
  272.6 8.3 %copy.96 = f32[8,16,2,7168]{3,1,2,0:T(8,128)} copy(f32[8,16,2,7168]{3,2,1,0:T(2,128)} %reshape.239) | data formatting | bytes 14680064 | tf_op jit(solution)/shard_map/reshape | solution.py:41
  280.9 8.5 %copy.103 = bf16[256,16,448]{0,1,2:T(8,128)(2,1)} copy(bf16[256,16,448]{2,1,0:T(8,128)(2,1)} %reshape.233) | data formatting | bytes 7340032 | tf_op jit(solution)/shard_map/reshape | solution.py:17
  289.4 8.9 %all-to-all-start.7 = ((f32[1,16,2]{2,0,1:T(1,128)}), f32[1,16,2]{2,0,1:T(1,128)S(1)}, u32[]{:S(2)}, u32[]{:S(2)}) async-start(f32[1,16,2]{2,0,1:T(1,128)} %bitcast.76), calls=%async_computation.9 | async-start | bytes 16384 | tf_op jit(solution)/shard_map/all_to_all | solution.py:123
  304.8 7.3 %all-to-all-start.10 = ((bf16[16,256,448]{1,2,0:T(8,128)(2,1)}), bf16[16,256,448]{1,2,0:T(8,128)(2,1)}, u32[]{:S(2)}, u32[]{:S(2)}) async-start(bf16[16,256,448]{1,2,0:T(8,128)(2,1)} %copy.104), calls=%async_computation.12 | async-start | bytes 7340032 | tf_op jit(solution)/shard_map/all_to_all | solution.py:144
  312.1 5.1 %convolution_convert_fusion.1 = bf16[7168,256]{1,0:T(8,128)(2,1)} fusion(bf16[256,7168]{1,0:T(8,128)(2,1)} %reshape.236, bf16[256,256]{0,1:T(8,128)(2,1)S(1)} %get-tuple-element.39), kind=kOutput, calls=%fused_computation.5 | convolution fusion | flops 941359104 | bytes 7471104 | tf_op jit(solution)/shard_map/rd,rh->dh/dot_general | solution.py:36
  317.2 39.1 %all-to-all-done.10 = bf16[16,256,448]{1,2,0:T(8,128)(2,1)} async-done(((bf16[16,256,448]{1,2,0:T(8,128)(2,1)}), bf16[16,256,448]{1,2,0:T(8,128)(2,1)}, u32[]{:S(2)}, u32[]{:S(2)}) %all-to-all-start.10) | async-done | bytes 3670048 | tf_op jit(solution)/shard_map/all_to_all | solution.py:144
  356.3 8.1 %all-to-all-start.8 = ((bf16[16,448,256]{2,1,0:T(8,128)(2,1)}), bf16[16,448,256]{2,1,0:T(8,128)(2,1)}, u32[]{:S(2)}, u32[]{:S(2)}) async-start(bf16[16,448,256]{2,1,0:T(8,128)(2,1)} %bitcast.72), calls=%async_computation.10 | async-start | bytes 7340032 | tf_op jit(solution)/shard_map/all_to_all | solution.py:142
  364.4 5.1 convolution_convert_fusion
  369.5 41.6 %all-to-all-done.8 = bf16[16,448,256]{2,1,0:T(8,128)(2,1)} async-done(((bf16[16,448,256]{2,1,0:T(8,128)(2,1)}), bf16[16,448,256]{2,1,0:T(8,128)(2,1)}, u32[]{:S(2)}, u32[]{:S(2)}) %all-to-all-start.8) | async-done | bytes 3670048 | tf_op jit(solution)/shard_map/all_to_all | solution.py:142
  411.0 9.3 %all-to-all-start.9 = ((bf16[16,448,256]{2,1,0:T(8,128)(2,1)}), bf16[16,448,256]{2,1,0:T(8,128)(2,1)}, u32[]{:S(2)}, u32[]{:S(2)}) async-start(bf16[16,448,256]{2,1,0:T(8,128)(2,1)} %bitcast.71), calls=%async_computation.11 | async-start | bytes 7340032 | tf_op jit(solution)/shard_map/all_to_all | solution.py:143
  426.3 38.1 %all-to-all-done.9 = bf16[16,448,256]{2,1,0:T(8,128)(2,1)} async-done(((bf16[16,448,256]{2,1,0:T(8,128)(2,1)}), bf16[16,448,256]{2,1,0:T(8,128)(2,1)}, u32[]{:S(2)}, u32[]{:S(2)}) %all-to-all-start.9) | async-done | bytes 3670048 | tf_op jit(solution)/shard_map/all_to_all | solution.py:143
  464.4 7.9 %all-to-all-start.6 = ((f32[1,16,2,7168]{3,2,0,1:T(2,128)}), f32[1,16,2,7168]{3,2,0,1:T(2,128)S(1)}, u32[]{:S(2)}, u32[]{:S(2)}) async-start(f32[1,16,2,7168]{3,2,0,1:T(2,128)} %copy.97), calls=%async_computation.7 | async-start | bytes 1835008 | tf_op jit(solution)/shard_map/all_to_all | solution.py:122
  491.4 8.5 %convolution_convert_fusion.2 = bf16[256,7168]{1,0:T(8,128)(2,1)} fusion(f32[32,256]{1,0:T(8,128)S(1)} %convert_reduce_fusion, f32[32,7168]{1,0:T(8,128)} %reshape.240), kind=kOutput, calls=%fused_computation.6 | convolution fusion | flops 706478080 | bytes 4620288 | tf_op jit(solution)/shard_map/qt,qd->td/dot_general | solution.py:125
  (93 shorter events, 69.6 us)
Async XLA Ops:
  7.2 44.6 %copy-start = (bf16[8,448,256]{2,1,0:T(8,128)(2,1)S(1)}, bf16[8,448,256]{2,1,0:T(8,128)(2,1)}, u32[]{:S(2)}) copy-start(bf16[8,448,256]{2,1,0:T(8,128)(2,1)} %param.16) | copy-start | bytes 5505028
  7.2 199.7 %all-gather.8.cloned.1.call-start = ((), (), s32[]{:S(2)}) async-start(), calls=%async_computation.16 | async-start | bytes 4128768 | tf_op jit(solution)/shard_map/all_gather | solution.py:108
  23.9 21.2 %copy-start.6 = (bf16[256,8]{0,1:T(8,128)(2,1)S(1)}, bf16[256,8]{0,1:T(8,128)(2,1)}, u32[]{:S(2)}) copy-start(bf16[256,8]{0,1:T(8,128)(2,1)} %param.12) | copy-start | bytes 12292
  24.0 26.9 %copy-start.5 = (s32[256,2]{0,1:T(2,128)S(1)}, s32[256,2]{0,1:T(2,128)}, u32[]{:S(2)}) copy-start(s32[256,2]{0,1:T(2,128)} %param.14) | copy-start | bytes 6148
  46.2 16.1 %all-to-all-start = ((bf16[16,1,2]{2,1,0:T(2,128)(2,1)}), bf16[16,1,2]{2,1,0:T(2,128)(2,1)S(1)}, u32[]{:S(2)}, u32[]{:S(2)}) async-start(bf16[16,1,2]{2,1,0:T(2,128)(2,1)} %all_to_all.48), calls=%async_computation | async-start | bytes 16384 | tf_op jit(solution)/shard_map/all_to_all | solution.py:104
  62.3 15.7 %all-to-all-start.1 = ((bf16[16,2,7168]{2,1,0:T(2,128)(2,1)}), bf16[16,2,7168]{2,1,0:T(2,128)(2,1)S(1)}, u32[]{:S(2)}, u32[]{:S(2)}) async-start(bf16[16,2,7168]{2,1,0:T(2,128)(2,1)} %reshape.232), calls=%async_computation.1 | async-start | bytes 917504 | tf_op jit(solution)/shard_map/all_to_all | solution.py:103
  78.0 0.8 copy-start.4
  78.8 51.4 %all-to-all-start.5 = ((bf16[16,448,256]{2,1,0:T(8,128)(2,1)}), bf16[16,448,256]{2,1,0:T(8,128)(2,1)}, u32[]{:S(2)}, u32[]{:S(2)}) async-start(bf16[16,448,256]{2,1,0:T(8,128)(2,1)} %get-tuple-element.44), calls=%async_computation.5 | async-start | bytes 7340032 | tf_op jit(solution)/shard_map/all_to_all | solution.py:95
  84.6 130.6 %all-gather.6.cloned.1.call-start = ((), (), s32[]{:S(2)}) async-start(), calls=%async_computation.15 | async-start | bytes 4128768 | tf_op jit(solution)/shard_map/all_gather | solution.py:109
  130.2 9.1 %copy-start.3 = (bf16[8,256,448]{1,2,0:T(8,128)(2,1)S(1)}, bf16[8,256,448]{1,2,0:T(8,128)(2,1)}, u32[]{:S(2)}) copy-start(bf16[8,256,448]{1,2,0:T(8,128)(2,1)} %param.17) | copy-start | bytes 5505028
  130.2 54.6 %all-to-all-start.4 = ((bf16[16,448,256]{2,1,0:T(8,128)(2,1)}), bf16[16,448,256]{2,1,0:T(8,128)(2,1)}, u32[]{:S(2)}, u32[]{:S(2)}) async-start(bf16[16,448,256]{2,1,0:T(8,128)(2,1)} %get-tuple-element.43), calls=%async_computation.4 | async-start | bytes 7340032 | tf_op jit(solution)/shard_map/all_to_all | solution.py:96
  184.7 54.4 %all-to-all-start.2 = ((bf16[16,256,448]{1,2,0:T(8,128)(2,1)}), bf16[16,256,448]{1,2,0:T(8,128)(2,1)}, u32[]{:S(2)}, u32[]{:S(2)}) async-start(bf16[16,256,448]{1,2,0:T(8,128)(2,1)} %broadcast_select_fusion.2), calls=%async_computation.2 | async-start | bytes 7340032 | tf_op jit(solution)/shard_map/all_to_all | solution.py:97
  193.5 95.9 %reduce-scatter.5.cloned.1.call-start = ((), (), s32[]{:S(2)}) async-start(), calls=%async_computation.14 | async-start | bytes 73728 | tf_op jit(solution)/shard_map/reduce_scatter | solution.py:119
  224.9 4.8 copy-start.2
  254.4 169.1 %reduce-scatter.3.cloned.1.call-start = ((), (), s32[]{:S(2)}) async-start(), calls=%async_computation.13 | async-start | bytes 8257536 | tf_op jit(solution)/shard_map/reduce_scatter | solution.py:118
  289.4 15.4 %all-to-all-start.7 = ((f32[1,16,2]{2,0,1:T(1,128)}), f32[1,16,2]{2,0,1:T(1,128)S(1)}, u32[]{:S(2)}, u32[]{:S(2)}) async-start(f32[1,16,2]{2,0,1:T(1,128)} %bitcast.76), calls=%async_computation.9 | async-start | bytes 16384 | tf_op jit(solution)/shard_map/all_to_all | solution.py:123
  304.8 51.5 %all-to-all-start.10 = ((bf16[16,256,448]{1,2,0:T(8,128)(2,1)}), bf16[16,256,448]{1,2,0:T(8,128)(2,1)}, u32[]{:S(2)}, u32[]{:S(2)}) async-start(bf16[16,256,448]{1,2,0:T(8,128)(2,1)} %copy.104), calls=%async_computation.12 | async-start | bytes 7340032 | tf_op jit(solution)/shard_map/all_to_all | solution.py:144
  356.3 54.7 %all-to-all-start.8 = ((bf16[16,448,256]{2,1,0:T(8,128)(2,1)}), bf16[16,448,256]{2,1,0:T(8,128)(2,1)}, u32[]{:S(2)}, u32[]{:S(2)}) async-start(bf16[16,448,256]{2,1,0:T(8,128)(2,1)} %bitcast.72), calls=%async_computation.10 | async-start | bytes 7340032 | tf_op jit(solution)/shard_map/all_to_all | solution.py:142
  411.0 53.4 %all-to-all-start.9 = ((bf16[16,448,256]{2,1,0:T(8,128)(2,1)}), bf16[16,448,256]{2,1,0:T(8,128)(2,1)}, u32[]{:S(2)}, u32[]{:S(2)}) async-start(bf16[16,448,256]{2,1,0:T(8,128)(2,1)} %bitcast.71), calls=%async_computation.11 | async-start | bytes 7340032 | tf_op jit(solution)/shard_map/all_to_all | solution.py:143
  464.4 25.4 %all-to-all-start.6 = ((f32[1,16,2,7168]{3,2,0,1:T(2,128)}), f32[1,16,2,7168]{3,2,0,1:T(2,128)S(1)}, u32[]{:S(2)}, u32[]{:S(2)}) async-start(f32[1,16,2,7168]{3,2,0,1:T(2,128)} %copy.97), calls=%async_computation.7 | async-start | bytes 1835008 | tf_op jit(solution)/shard_map/all_to_all | solution.py:122
  488.2 11.7 %copy-start.1 = (bf16[8,448,256]{2,1,0:T(8,128)(2,1)S(1)}, bf16[8,448,256]{2,1,0:T(8,128)(2,1)}, u32[]{:S(2)}) copy-start(bf16[8,448,256]{2,1,0:T(8,128)(2,1)} %param.16) | copy-start | bytes 5505028
Sparse Core Ops, SparseCore 0:
  45.1 26.5 all-gather.7
  87.7 29.2 all-gather.5
  254.6 30.1 reduce-scatter.4
  287.0 47.4 reduce-scatter.2
where the time goes:
time: 516 us; the launch traced here: 507 us
  waiting for transfers between devices  210 us (41%)
  starting transfers between devices  77.3 us (15%)
  local copies, waits for them, and re-layouts  74.5 us (14%)
  matrix products  72.8 us (14%)
  blocking collectives  30.7 us (6%)
  other arithmetic  27.2 us (5%)
  between operations  14.2 us (3%)
    all_to_all x1, waiting for transfers between devices, local(): lax.all_to_all(copy_gate, 'dev', split_axis=0, concat_axis=0, tiled=True)  44.8 us
    all_to_all x1, waiting for transfers between devices, local(): lax.all_to_all(send_gate, 'dev', split_axis=0, concat_axis=0, tiled=True)  41.6 us
    all_to_all x1, waiting for transfers between devices, local(): lax.all_to_all(send_down, 'dev', split_axis=0, concat_axis=0, tiled=True)  39.1 us
    all_to_all x1, waiting for transfers between devices, local(): lax.all_to_all(copy_up, 'dev', split_axis=0, concat_axis=0, tiled=True)  38.6 us
    all_to_all x1, waiting for transfers between devices, local(): lax.all_to_all(send_up, 'dev', split_axis=0, concat_axis=0, tiled=True)  38.1 us
    reshape x2, local copies, waits for them, and re-layouts, expert_pass(): dy_split = dy_piece.reshape(-1, slot_count, model_width // slot_count)  18.1 us
    reshape x2, local copies, waits for them, and re-layouts, expert_pass(): row_acc = row_terms.reshape(lead_count, slot_count, -1, model_width)  18 us
    all_to_all x1, blocking collectives, local(): lax.all_to_all(x_send, 'dev', split_axis=0, concat_axis=0, tiled=True)  17.7 us
  transfers between devices with their start and end apart: 14, of which 7 were waited for; matrix products, arithmetic and copies ran while one was open for 25% of the time, Pallas kernels for 0%

commit v1 on v0

--- a/solution.py
+++ b/solution.py
@@ -6,6 +6,27 @@
 EXPERTS = 256
 TOP = 8
 CAP = 2
+
+
+def gather_around(x, axis, dim):
+    size, index, width = (lax.axis_size(axis), lax.axis_index(axis), x.shape[dim])
+    right = [(i, (i + 1) % size) for i in range(size)]
+    left = [(i, (i - 1) % size) for i in range(size)]
+    result = jnp.zeros((*x.shape[:dim], size * width, *x.shape[dim + 1 :]), x.dtype)
+    result = lax.dynamic_update_slice_in_dim(result, x, index * width, axis=dim)
+    from_left = from_right = x
+    middle = size // 2
+    for hop in range(1, middle + 1):
+        from_left = lax.ppermute(from_left, axis, right)
+        result = lax.dynamic_update_slice_in_dim(
+            result, from_left, (index - hop) % size * width, axis=dim
+        )
+        if hop < size - middle:
+            from_right = lax.ppermute(from_right, axis, left)
+            result = lax.dynamic_update_slice_in_dim(
+                result, from_right, (index + hop) % size * width, axis=dim
+            )
+    return result
 
 
 def expert_pass(pieces, slot_gate, slot_up, slot_down):
@@ -107,7 +128,7 @@
         (
             lax.all_gather(got_x[None], "node", axis=0, tiled=True),
             lax.all_gather(got_dy[None], "node", axis=0, tiled=True),
-            lax.all_gather(got_gate[None], "node", axis=0, tiled=True),
+            gather_around(got_gate[None], "node", 0),
         ),
         slot_gate,
         slot_up,

time: 516 us -> 525 us (1.017)
  waiting for transfers between devices: 210 us -> 225 us
  blocking collectives: 30.7 us -> 17.7 us
  starting transfers between devices: 77.3 us -> 82.8 us
    all_gather x1 -> x0, blocking collectives: 13 us -> none  [local(): lax.all_gather(got_gate[None], 'node', axis=0, tiled=True)]
    ppermute x0 -> x7, starting transfers between devices: none -> 6.45 us  [the longest x3 5.59 us: gather_around(): from_right = lax.ppermute(from_right, axis, left)]
    all_to_all x1, waiting for transfers between devices: 38.6 us -> 44.8 us  [local(): lax.all_to_all(copy_up, 'dev', split_axis=0, concat_axis=0, tiled=True)]
    all_to_all x1, waiting for transfers between devices: 41.6 us -> 47.7 us  [local(): lax.all_to_all(send_gate, 'dev', split_axis=0, concat_axis=0, tiled=True)]
    all_to_all x1, waiting for transfers between devices: 44.8 us -> 38.7 us  [local(): lax.all_to_all(copy_gate, 'dev', split_axis=0, concat_axis=0, tiled=True)]
  transfers between devices with their start and end apart: 14 -> 21, of which waited for: 7 -> 15; matrix products, arithmetic and copies ran while one was open for 25% -> 25% of each run, Pallas kernels for 0% -> 0%
where the time goes in v1:
time: 525 us; the launch traced here: 515 us
  waiting for transfers between devices  225 us (43%)
  starting transfers between devices  82.8 us (16%)
  local copies, waits for them, and re-layouts  75.1 us (14%)
  matrix products  72.9 us (14%)
  other arithmetic  26.9 us (5%)
  blocking collectives  17.7 us (3%)
  between operations  14.4 us (3%)
    all_to_all x1, waiting for transfers between devices, local(): lax.all_to_all(send_gate, 'dev', split_axis=0, concat_axis=0, tiled=True)  47.7 us
    all_to_all x1, waiting for transfers between devices, local(): lax.all_to_all(copy_up, 'dev', split_axis=0, concat_axis=0, tiled=True)  44.8 us
    all_to_all x1, waiting for transfers between devices, local(): lax.all_to_all(send_down, 'dev', split_axis=0, concat_axis=0, tiled=True)  40.4 us
    all_to_all x1, waiting for transfers between devices, local(): lax.all_to_all(copy_gate, 'dev', split_axis=0, concat_axis=0, tiled=True)  38.7 us
    all_to_all x1, waiting for transfers between devices, local(): lax.all_to_all(send_up, 'dev', split_axis=0, concat_axis=0, tiled=True)  35.6 us
    reshape x2, local copies, waits for them, and re-layouts, expert_pass(): row_acc = row_terms.reshape(lead_count, slot_count, -1, model_width)  18 us
    reshape x2, local copies, waits for them, and re-layouts, expert_pass(): dy_split = dy_piece.reshape(-1, slot_count, model_width // slot_count)  18 us
    all_to_all x1, blocking collectives, local(): lax.all_to_all(x_send, 'dev', split_axis=0, concat_axis=0, tiled=True)  17.7 us
  transfers between devices with their start and end apart: 21, of which 15 were waited for; matrix products, arithmetic and copies ran while one was open for 25% of the time, Pallas kernels for 0%

profile of v1, /device:TPU:14, one launch (start us, length us, event | category | flops | bytes accessed | tf_op | source)
XLA Modules:
  0.0 515.2 jit_solution(11072962703943981770)
XLA Ops:
  8.9 9.2 %select_reduce_fusion = (s32[256,8]{1,0:T(8,128)S(1)}, s32[256,8]{1,0:T(8,128)S(1)}) fusion(s32[256]{0:T(256)S(1)} %bitcast.79, s32[256,8]{1,0:T(8,128)S(1)} %copy.99, s32[256]{0:T(256)S(1)} %bitcast.78), kind=kLoop, calls=%fused_computation.21 | loop fusion | flops 2617344 | bytes 26624 | tf_op jit(solution)/shard_map/reduce_sum | solution.py:75
  18.4 4.5 reduce-window.15
  27.2 17.7 %all_to_all.60 = bf16[16,2,7168]{2,1,0:T(2,128)(2,1)} all-to-all(bf16[16,2,7168]{2,1,0:T(2,128)(2,1)S(1)} %reshape.235), channel_id=1, replica_groups=mesh['node'=8,'dev'=16] {'dev'}, dimensions={0} | all-to-all | bytes 917504 | tf_op jit(solution)/shard_map/all_to_all | solution.py:123
  46.2 4.7 all-to-all-start
  62.2 7.3 %all-to-all-start.1 = ((bf16[16,2,7168]{2,1,0:T(2,128)(2,1)}), bf16[16,2,7168]{2,1,0:T(2,128)(2,1)S(1)}, u32[]{:S(2)}, u32[]{:S(2)}) async-start(bf16[16,2,7168]{2,1,0:T(2,128)(2,1)} %reshape.232), calls=%async_computation.1 | async-start | bytes 917504 | tf_op jit(solution)/shard_map/all_to_all | solution.py:124
  69.5 6.9 %broadcast_select_fusion.1 = (bf16[16,448,256]{2,1,0:T(8,128)(2,1)}, bf16[16,448,256]{2,1,0:T(8,128)(2,1)}) fusion(bf16[16,448,256]{2,1,0:T(8,128)(2,1)} %gather_fusion.1, pred[16]{0:T(512)(128)(4,1)S(1)} %compare_and_fusion, bf16[16,448,256]{2,1,0:T(8,128)(2,1)} %gather_fusion.2), kind=kLoop, calls=%fused_computation.19 | loop fusion | flops 3670016 | bytes 14680080 | tf_op jit(solution)/shard_map/jit(_take)/select_n | solution.py:113
  78.7 5.8 %all-to-all-start.4 = ((bf16[16,448,256]{2,1,0:T(8,128)(2,1)}), bf16[16,448,256]{2,1,0:T(8,128)(2,1)}, u32[]{:S(2)}, u32[]{:S(2)}) async-start(bf16[16,448,256]{2,1,0:T(8,128)(2,1)} %get-tuple-element.38), calls=%async_computation.4 | async-start | bytes 7340032 | tf_op jit(solution)/shard_map/all_to_all | solution.py:117
  85.2 44.8 %all-to-all-done.4 = bf16[16,448,256]{2,1,0:T(8,128)(2,1)} async-done(((bf16[16,448,256]{2,1,0:T(8,128)(2,1)}), bf16[16,448,256]{2,1,0:T(8,128)(2,1)}, u32[]{:S(2)}, u32[]{:S(2)}) %all-to-all-start.4) | async-done | bytes 3670048 | tf_op jit(solution)/shard_map/all_to_all | solution.py:117
  130.0 9.0 %all-to-all-start.5 = ((bf16[16,448,256]{2,1,0:T(8,128)(2,1)}), bf16[16,448,256]{2,1,0:T(8,128)(2,1)}, u32[]{:S(2)}, u32[]{:S(2)}) async-start(bf16[16,448,256]{2,1,0:T(8,128)(2,1)} %get-tuple-element.39), calls=%async_computation.5 | async-start | bytes 7340032 | tf_op jit(solution)/shard_map/all_to_all | solution.py:116
  145.9 38.7 %all-to-all-done.5 = bf16[16,448,256]{2,1,0:T(8,128)(2,1)} async-done(((bf16[16,448,256]{2,1,0:T(8,128)(2,1)}), bf16[16,448,256]{2,1,0:T(8,128)(2,1)}, u32[]{:S(2)}, u32[]{:S(2)}) %all-to-all-start.5) | async-done | bytes 3670048 | tf_op jit(solution)/shard_map/all_to_all | solution.py:116
  184.6 8.8 %all-to-all-start.2 = ((bf16[16,256,448]{1,2,0:T(8,128)(2,1)}), bf16[16,256,448]{1,2,0:T(8,128)(2,1)}, u32[]{:S(2)}, u32[]{:S(2)}) async-start(bf16[16,256,448]{1,2,0:T(8,128)(2,1)} %broadcast_select_fusion.2), calls=%async_computation.2 | async-start | bytes 7340032 | tf_op jit(solution)/shard_map/all_to_all | solution.py:118
  206.4 8.4 %reshape.236 = bf16[256,7168]{1,0:T(8,128)(2,1)} reshape(bf16[128,2,7168]{2,1,0:T(2,128)(2,1)} %all-gather.7.cloned.1.call-done) | data formatting | bytes 7340032 | tf_op jit(solution)/shard_map/reshape | solution.py:37
  214.8 9.6 %reshape.233 = bf16[256,16,448]{2,1,0:T(8,128)(2,1)} reshape(bf16[128,2,7168]{2,1,0:T(2,128)(2,1)} %all-gather.5.cloned.1.call-done) | data formatting | bytes 7340032 | tf_op jit(solution)/shard_map/reshape | solution.py:38
  224.4 4.8 fusion.61
  232.9 5.9 %all-to-all-done.2 = bf16[16,256,448]{1,2,0:T(8,128)(2,1)} async-done(((bf16[16,256,448]{1,2,0:T(8,128)(2,1)}), bf16[16,256,448]{1,2,0:T(8,128)(2,1)}, u32[]{:S(2)}, u32[]{:S(2)}) %all-to-all-start.2) | async-done | bytes 3670048 | tf_op jit(solution)/shard_map/all_to_all | solution.py:118
  238.9 8.3 %multiply_reduce_fusion = (f32[256]{0:T(256)S(1)}, bf16[256,256]{0,1:T(8,128)(2,1)S(1)}, bf16[256,256]{0,1:T(8,128)(2,1)S(1)}) fusion(f32[256,256]{0,1:T(8,128)S(1)} %fusion.61, f32[256,256]{0,1:T(8,128)S(1)} %fusion.62, f32[256]{0:T(256)S(1)} %reshape.245, bf16[16,256,448]{1,2,0:T(8,128)(2,1)} %all-to-all-done.2, bf16[256,16,448]{2,1,0:T(8,128)(2,1)} %reshape.233), kind=kOutput, calls=%fused_computation.32 | convolution fusion | flops 940637952 | bytes 8128512 | tf_op jit(solution)/shard_map/rsk,shk->rh/dot_general | solution.py:42
  247.2 6.2 %fusion.63 = f32[256,7168]{1,0:T(8,128)} fusion(bf16[256,256]{0,1:T(8,128)(2,1)S(1)} %get-tuple-element.34, bf16[7168,256]{1,0:T(8,128)(2,1)} %bitcast.11), kind=kOutput, calls=%fused_computation.112 | convolution fusion | flops 939524096 | bytes 11141120 | tf_op jit(solution)/shard_map/rh,dh->rd/dot_general | solution.py:53
  254.2 8.3 %convolution_add_fusion = f32[256,7168]{1,0:T(8,128)} fusion(f32[256,7168]{1,0:T(8,128)} %fusion.63, bf16[256,256]{0,1:T(8,128)(2,1)S(1)} %get-tuple-element.35, bf16[7168,256]{1,0:T(8,128)(2,1)} %bitcast.10), kind=kOutput, calls=%fused_computation.3 | convolution fusion | flops 941359104 | bytes 18481152 | tf_op jit(solution)/shard_map/rh,dh->rd/dot_general | solution.py:54
  262.5 9.7 %reshape.239 = f32[8,16,2,7168]{3,2,1,0:T(2,128)} reshape(f32[256,7168]{1,0:T(8,128)} %convolution_add_fusion) | data formatting | bytes 14680064 | tf_op jit(solution)/shard_map/reshape | solution.py:62
  272.3 8.2 %copy.114 = f32[8,16,2,7168]{3,1,2,0:T(8,128)} copy(f32[8,16,2,7168]{3,2,1,0:T(2,128)} %reshape.239) | data formatting | bytes 14680064 | tf_op jit(solution)/shard_map/reshape | solution.py:62
  284.6 7.4 %all-to-all-start.7 = ((f32[1,16,2]{2,0,1:T(1,128)}), f32[1,16,2]{2,0,1:T(1,128)S(1)}, u32[]{:S(2)}, u32[]{:S(2)}) async-start(f32[1,16,2]{2,0,1:T(1,128)} %bitcast.77), calls=%async_computation.9 | async-start | bytes 16384 | tf_op jit(solution)/shard_map/all_to_all | solution.py:144
  292.0 5.1 convolution_convert_fusion.1
  298.1 6.3 %all-to-all-start.8 = ((bf16[16,448,256]{2,1,0:T(8,128)(2,1)}), bf16[16,448,256]{2,1,0:T(8,128)(2,1)}, u32[]{:S(2)}, u32[]{:S(2)}) async-start(bf16[16,448,256]{2,1,0:T(8,128)(2,1)} %bitcast.73), calls=%async_computation.10 | async-start | bytes 7340032 | tf_op jit(solution)/shard_map/all_to_all | solution.py:163
  304.4 5.2 %convolution_convert_fusion = bf16[7168,256]{1,0:T(8,128)(2,1)} fusion(bf16[256,7168]{1,0:T(8,128)(2,1)} %reshape.236, bf16[256,256]{0,1:T(8,128)(2,1)S(1)} %get-tuple-element.35), kind=kOutput, calls=%fused_computation.4 | convolution fusion | flops 941359104 | bytes 7471104 | tf_op jit(solution)/shard_map/rd,rh->dh/dot_general | solution.py:58
  309.6 47.7 %all-to-all-done.8 = bf16[16,448,256]{2,1,0:T(8,128)(2,1)} async-done(((bf16[16,448,256]{2,1,0:T(8,128)(2,1)}), bf16[16,448,256]{2,1,0:T(8,128)(2,1)}, u32[]{:S(2)}, u32[]{:S(2)}) %all-to-all-start.8) | async-done | bytes 3670048 | tf_op jit(solution)/shard_map/all_to_all | solution.py:163
  357.2 8.8 %all-to-all-start.9 = ((bf16[16,448,256]{2,1,0:T(8,128)(2,1)}), bf16[16,448,256]{2,1,0:T(8,128)(2,1)}, u32[]{:S(2)}, u32[]{:S(2)}) async-start(bf16[16,448,256]{2,1,0:T(8,128)(2,1)} %bitcast.72), calls=%async_computation.11 | async-start | bytes 7340032 | tf_op jit(solution)/shard_map/all_to_all | solution.py:164
  366.0 8.4 %copy.121 = bf16[256,16,448]{0,1,2:T(8,128)(2,1)} copy(bf16[256,16,448]{2,1,0:T(8,128)(2,1)} %reshape.233) | data formatting | bytes 7340032 | tf_op jit(solution)/shard_map/reshape | solution.py:38
  380.9 35.6 %all-to-all-done.9 = bf16[16,448,256]{2,1,0:T(8,128)(2,1)} async-done(((bf16[16,448,256]{2,1,0:T(8,128)(2,1)}), bf16[16,448,256]{2,1,0:T(8,128)(2,1)}, u32[]{:S(2)}, u32[]{:S(2)}) %all-to-all-start.9) | async-done | bytes 3670048 | tf_op jit(solution)/shard_map/all_to_all | solution.py:164
  416.5 9.0 %all-to-all-start.10 = ((bf16[16,256,448]{1,2,0:T(8,128)(2,1)}), bf16[16,256,448]{1,2,0:T(8,128)(2,1)}, u32[]{:S(2)}, u32[]{:S(2)}) async-start(bf16[16,256,448]{1,2,0:T(8,128)(2,1)} %copy.122), calls=%async_computation.12 | async-start | bytes 7340032 | tf_op jit(solution)/shard_map/all_to_all | solution.py:165
  431.5 40.4 %all-to-all-done.10 = bf16[16,256,448]{1,2,0:T(8,128)(2,1)} async-done(((bf16[16,256,448]{1,2,0:T(8,128)(2,1)}), bf16[16,256,448]{1,2,0:T(8,128)(2,1)}, u32[]{:S(2)}, u32[]{:S(2)}) %all-to-all-start.10) | async-done | bytes 3670048 | tf_op jit(solution)/shard_map/all_to_all | solution.py:165
  471.9 9.0 %all-to-all-start.6 = ((f32[1,16,2,7168]{3,2,0,1:T(2,128)}), f32[1,16,2,7168]{3,2,0,1:T(2,128)S(1)}, u32[]{:S(2)}, u32[]{:S(2)}) async-start(f32[1,16,2,7168]{3,2,0,1:T(2,128)} %copy.115), calls=%async_computation.7 | async-start | bytes 1835008 | tf_op jit(solution)/shard_map/all_to_all | solution.py:143
  499.9 8.5 %convolution_convert_fusion.2 = bf16[256,7168]{1,0:T(8,128)(2,1)} fusion(f32[32,256]{1,0:T(8,128)S(1)} %convert_reduce_fusion, f32[32,7168]{1,0:T(8,128)} %reshape.240), kind=kOutput, calls=%fused_computation.6 | convolution fusion | flops 706478080 | bytes 4620288 | tf_op jit(solution)/shard_map/qt,qd->td/dot_general | solution.py:146
  (123 shorter events, 82.5 us)
Async XLA Ops:
  7.2 44.6 %copy-start = (bf16[8,448,256]{2,1,0:T(8,128)(2,1)S(1)}, bf16[8,448,256]{2,1,0:T(8,128)(2,1)}, u32[]{:S(2)}) copy-start(bf16[8,448,256]{2,1,0:T(8,128)(2,1)} %param.16) | copy-start | bytes 5505028
  7.2 199.3 %all-gather.7.cloned.1.call-start = ((), (), s32[]{:S(2)}) async-start(), calls=%async_computation.16 | async-start | bytes 4128768 | tf_op jit(solution)/shard_map/all_gather | solution.py:129
  23.9 21.2 %copy-start.6 = (bf16[256,8]{0,1:T(8,128)(2,1)S(1)}, bf16[256,8]{0,1:T(8,128)(2,1)}, u32[]{:S(2)}) copy-start(bf16[256,8]{0,1:T(8,128)(2,1)} %param.12) | copy-start | bytes 12292
  24.0 26.9 %copy-start.5 = (s32[256,2]{0,1:T(2,128)S(1)}, s32[256,2]{0,1:T(2,128)}, u32[]{:S(2)}) copy-start(s32[256,2]{0,1:T(2,128)} %param.14) | copy-start | bytes 6148
  46.2 16.0 %all-to-all-start = ((bf16[16,1,2]{2,1,0:T(2,128)(2,1)}), bf16[16,1,2]{2,1,0:T(2,128)(2,1)S(1)}, u32[]{:S(2)}, u32[]{:S(2)}) async-start(bf16[16,1,2]{2,1,0:T(2,128)(2,1)} %all_to_all.48), calls=%async_computation | async-start | bytes 16384 | tf_op jit(solution)/shard_map/all_to_all | solution.py:125
  62.2 15.7 %all-to-all-start.1 = ((bf16[16,2,7168]{2,1,0:T(2,128)(2,1)}), bf16[16,2,7168]{2,1,0:T(2,128)(2,1)S(1)}, u32[]{:S(2)}, u32[]{:S(2)}) async-start(bf16[16,2,7168]{2,1,0:T(2,128)(2,1)} %reshape.232), calls=%async_computation.1 | async-start | bytes 917504 | tf_op jit(solution)/shard_map/all_to_all | solution.py:124
  77.9 0.8 copy-start.4
  78.7 51.3 %all-to-all-start.4 = ((bf16[16,448,256]{2,1,0:T(8,128)(2,1)}), bf16[16,448,256]{2,1,0:T(8,128)(2,1)}, u32[]{:S(2)}, u32[]{:S(2)}) async-start(bf16[16,448,256]{2,1,0:T(8,128)(2,1)} %get-tuple-element.38), calls=%async_computation.4 | async-start | bytes 7340032 | tf_op jit(solution)/shard_map/all_to_all | solution.py:117
  84.5 130.4 %all-gather.5.cloned.1.call-start = ((), (), s32[]{:S(2)}) async-start(), calls=%async_computation.15 | async-start | bytes 4128768 | tf_op jit(solution)/shard_map/all_gather | solution.py:130
  130.0 9.0 %copy-start.3 = (bf16[8,256,448]{1,2,0:T(8,128)(2,1)S(1)}, bf16[8,256,448]{1,2,0:T(8,128)(2,1)}, u32[]{:S(2)}) copy-start(bf16[8,256,448]{1,2,0:T(8,128)(2,1)} %param.17) | copy-start | bytes 5505028
  130.0 54.6 %all-to-all-start.5 = ((bf16[16,448,256]{2,1,0:T(8,128)(2,1)}), bf16[16,448,256]{2,1,0:T(8,128)(2,1)}, u32[]{:S(2)}, u32[]{:S(2)}) async-start(bf16[16,448,256]{2,1,0:T(8,128)(2,1)} %get-tuple-element.39), calls=%async_computation.5 | async-start | bytes 7340032 | tf_op jit(solution)/shard_map/all_to_all | solution.py:116
  184.6 54.3 %all-to-all-start.2 = ((bf16[16,256,448]{1,2,0:T(8,128)(2,1)}), bf16[16,256,448]{1,2,0:T(8,128)(2,1)}, u32[]{:S(2)}, u32[]{:S(2)}) async-start(bf16[16,256,448]{1,2,0:T(8,128)(2,1)} %broadcast_select_fusion.2), calls=%async_computation.2 | async-start | bytes 7340032 | tf_op jit(solution)/shard_map/all_to_all | solution.py:118
  193.3 91.3 %reduce-scatter.5.cloned.1.call-start = ((), (), s32[]{:S(2)}) async-start(), calls=%async_computation.14 | async-start | bytes 73728 | tf_op jit(solution)/shard_map/reduce_scatter | solution.py:140
  193.9 3.0 collective-permute-start
  193.9 3.1 collective-permute-start.1
  197.0 3.0 collective-permute-start.2
  197.1 3.0 collective-permute-start.3
  200.1 3.0 collective-permute-start.4
  200.2 4.3 collective-permute-start.5
  203.2 3.0 collective-permute-start.6
  224.4 4.8 copy-start.2
  254.1 174.6 %reduce-scatter.3.cloned.1.call-start = ((), (), s32[]{:S(2)}) async-start(), calls=%async_computation.13 | async-start | bytes 8257536 | tf_op jit(solution)/shard_map/reduce_scatter | solution.py:139
  284.6 13.5 %all-to-all-start.7 = ((f32[1,16,2]{2,0,1:T(1,128)}), f32[1,16,2]{2,0,1:T(1,128)S(1)}, u32[]{:S(2)}, u32[]{:S(2)}) async-start(f32[1,16,2]{2,0,1:T(1,128)} %bitcast.77), calls=%async_computation.9 | async-start | bytes 16384 | tf_op jit(solution)/shard_map/all_to_all | solution.py:144
  298.1 59.1 %all-to-all-start.8 = ((bf16[16,448,256]{2,1,0:T(8,128)(2,1)}), bf16[16,448,256]{2,1,0:T(8,128)(2,1)}, u32[]{:S(2)}, u32[]{:S(2)}) async-start(bf16[16,448,256]{2,1,0:T(8,128)(2,1)} %bitcast.73), calls=%async_computation.10 | async-start | bytes 7340032 | tf_op jit(solution)/shard_map/all_to_all | solution.py:163
  357.2 59.3 %all-to-all-start.9 = ((bf16[16,448,256]{2,1,0:T(8,128)(2,1)}), bf16[16,448,256]{2,1,0:T(8,128)(2,1)}, u32[]{:S(2)}, u32[]{:S(2)}) async-start(bf16[16,448,256]{2,1,0:T(8,128)(2,1)} %bitcast.72), calls=%async_computation.11 | async-start | bytes 7340032 | tf_op jit(solution)/shard_map/all_to_all | solution.py:164
  416.5 55.4 %all-to-all-start.10 = ((bf16[16,256,448]{1,2,0:T(8,128)(2,1)}), bf16[16,256,448]{1,2,0:T(8,128)(2,1)}, u32[]{:S(2)}, u32[]{:S(2)}) async-start(bf16[16,256,448]{1,2,0:T(8,128)(2,1)} %copy.122), calls=%async_computation.12 | async-start | bytes 7340032 | tf_op jit(solution)/shard_map/all_to_all | solution.py:165
  471.9 26.5 %all-to-all-start.6 = ((f32[1,16,2,7168]{3,2,0,1:T(2,128)}), f32[1,16,2,7168]{3,2,0,1:T(2,128)S(1)}, u32[]{:S(2)}, u32[]{:S(2)}) async-start(f32[1,16,2,7168]{3,2,0,1:T(2,128)} %copy.115), calls=%async_computation.7 | async-start | bytes 1835008 | tf_op jit(solution)/shard_map/all_to_all | solution.py:143
  496.8 11.7 %copy-start.1 = (bf16[8,448,256]{2,1,0:T(8,128)(2,1)S(1)}, bf16[8,448,256]{2,1,0:T(8,128)(2,1)}, u32[]{:S(2)}) copy-start(bf16[8,448,256]{2,1,0:T(8,128)(2,1)} %param.16) | copy-start | bytes 5505028
Sparse Core Ops, SparseCore 0:
  45.1 26.5 all-gather.6
  87.5 29.2 all-gather.4
  254.3 30.3 reduce-scatter.4
  286.9 47.3 reduce-scatter.2
